TPU v7x, 128 devices: a whole 4x4x4 slice. The times are simulated.
128 devices in a mesh: head: 4 (over z), page: 32 (over x, y, core).
Axes of the slice: x: 4, y: 4, z: 4, core: 2. Of those that a mesh axis runs over, the one named last changes fastest.
Arguments:
- hidden_in: bfloat16 [32, 1024, 1024], P('page', 'head'), may hold values from -6 to 6
- norm_gain: float32 [1024], replicated, may hold values from 0.1 to 1.9
- w_qkv: bfloat16 [1024, 3, 1024], P(None, None, 'head'), may hold values from -0.1875 to 0.1875
- w_out: bfloat16 [1024, 1024], P('head'), may hold values from -0.75 to 0.75
- cache_kv: bfloat16 [2, 64, 128, 1024], P(None, 'page', None, 'head'), may hold values from -110 to 110, as said below
- page_node: int32 [64], replicated, may hold values from 0 to 18, as said below
- page_fill: int32 [64], replicated, may hold values from 1 to 128
- node_parent: int32 [19], replicated, may hold values from 0 to 2, as said below
- tok_seg: int32 [32, 1024], P('page'), may hold values from 0 to 7, never falling along the last dimension, each value on 1 to 256 neighbouring positions
- req_leaf: int32 [32, 8], P('page'), may hold values from 3 to 18, as said below
Outputs:
- attn_out: bfloat16 [32, 1024, 1024], P('page', 'head')
Inputs may be any that keep to these rules, and one draw needn't show every extreme that they name: `cache_kv`: entries of the cache; keys and values. `page_node`: every node owns at least one page. `node_parent`: node 0 is the root and its own parent; nodes 1 to 2 have parent 0; the others have a parent among nodes 1 to 2, and each of those has a child. `req_leaf`: each request names a lowest-level node; every lowest-level node is named by some request.
All inputs are finite; a program needn't handle non-finite values.
Results may differ from a plain program's by a relative error of at most 0.018.
Values may be sent and summed in bfloat16 or wider, within the bound.
No kernel may reach another device: no remote copies, remote signals or barrier semaphores. Data moves between devices by JAX's collectives and lax.ppermute only.
A program may use at most 64 MiB of HBM per device.

v0:
```python
import math
import jax
import jax.numpy as jnp
from jax import lax
from jax.sharding import PartitionSpec as P

HD = 64
EPSILON = 1e-06
FLOOR_SCORE = -1e30


def lookup(indices, lookup_table):
    matches = indices[:, None] == jnp.arange(lookup_table.shape[0], dtype=jnp.int32)[None, :]
    return jnp.sum(jnp.where(matches, lookup_table[None, :], 0), axis=1)


def shards(
    hidden_in,
    norm_gain,
    w_qkv,
    w_out,
    cache_kv,
    page_node,
    page_fill,
    node_parent,
    tok_seg,
    req_leaf,
):
    widened = hidden_in[0].astype(jnp.float32)
    normed = (
        widened
        * lax.rsqrt(jnp.mean(widened * widened, axis=1, keepdims=True) + EPSILON)
        * norm_gain
    ).astype(jnp.bfloat16)
    model_width = widened.shape[1]
    group_width = w_qkv.shape[2]
    head_size = HD
    group_heads = group_width // head_size
    weight_flat = w_qkv.reshape(model_width, 3 * group_width)
    projected = jnp.dot(
        lax.all_gather(normed, "head", axis=0, tiled=True),
        weight_flat,
        preferred_element_type=jnp.float32,
    ).astype(jnp.bfloat16)
    queries_all = projected.shape[0]
    queries = projected[:, :group_width].reshape(queries_all, group_heads, head_size)
    key_new = projected[:, group_width : 2 * group_width].reshape(
        queries_all, group_heads, head_size
    )
    value_new = projected[:, 2 * group_width :].reshape(queries_all, group_heads, head_size)
    score_scale = head_size ** (-0.5)
    segment = tok_seg[0]
    leaf_node = lookup(segment, req_leaf[0])
    upper_node = lookup(leaf_node, node_parent)
    root_node = lookup(upper_node, node_parent)
    position = jnp.arange(queries_all, dtype=jnp.int32)
    block_rows = min(queries_all, 512)

    def suffix_block(first):
        query_rows = lax.dynamic_slice_in_dim(queries, first, block_rows, 0)
        segment_rows = lax.dynamic_slice_in_dim(segment, first, block_rows, 0)
        position_rows = first + jnp.arange(block_rows, dtype=jnp.int32)
        visible = (segment_rows[:, None] == segment[None, :]) & (
            position[None, :] <= position_rows[:, None]
        )
        scores = (
            jnp.einsum("qhd,khd->hqk", query_rows, key_new, preferred_element_type=jnp.float32)
            * score_scale
        )
        scores = jnp.where(visible[None], scores, FLOOR_SCORE)
        row_max = jnp.max(scores, axis=2)
        weights = jnp.where(visible[None], jnp.exp(scores - row_max[:, :, None]), 0.0)
        row_sum = jnp.sum(weights, axis=2)
        weighted = jnp.einsum(
            "hqk,khd->hqd",
            weights.astype(jnp.bfloat16),
            value_new,
            preferred_element_type=jnp.float32,
        )
        return (row_max, row_sum, weighted)

    block_starts = jnp.arange(0, queries_all, block_rows, dtype=jnp.int32)
    block_max, block_sum, block_weighted = lax.map(suffix_block, block_starts)
    initial = (
        jnp.transpose(block_max, (1, 0, 2)).reshape(group_heads, queries_all),
        jnp.transpose(block_sum, (1, 0, 2)).reshape(group_heads, queries_all),
        jnp.transpose(block_weighted, (1, 0, 2, 3)).reshape(group_heads, queries_all, head_size),
    )
    page_len = cache_kv.shape[2]
    page_slot = jnp.arange(page_len, dtype=jnp.int32)
    shard_piece = lax.all_gather(cache_kv, "page", axis=1, tiled=True)
    piece_pages = shard_piece.shape[1]
    group_pages = math.gcd(piece_pages, 4)
    step_count = piece_pages // group_pages
    block_keys = group_pages * page_len
    key_blocks = shard_piece[0].reshape(step_count, block_keys, group_heads, head_size)
    value_blocks = shard_piece[1].reshape(step_count, block_keys, group_heads, head_size)
    key_nodes = jnp.repeat(page_node, page_len).reshape(step_count, block_keys)
    key_valid = (page_slot[None, :] < page_fill[:, None]).reshape(step_count, block_keys)

    def one_step(partial_value, inputs):
        row_max, row_sum, weighted = partial_value
        key_block, value_block, node_block, valid_block = inputs
        visible = (
            (node_block[None, :] == leaf_node[:, None])
            | (node_block[None, :] == upper_node[:, None])
            | (node_block[None, :] == root_node[:, None])
        ) & valid_block[None, :]
        scores = (
            jnp.einsum("qhd,khd->hqk", queries, key_block, preferred_element_type=jnp.float32)
            * score_scale
        )
        scores = jnp.where(visible[None], scores, FLOOR_SCORE)
        new_max = jnp.maximum(row_max, jnp.max(scores, axis=2))
        rescale = jnp.exp(row_max - new_max)
        weights = jnp.where(visible[None], jnp.exp(scores - new_max[:, :, None]), 0.0)
        row_sum = row_sum * rescale + jnp.sum(weights, axis=2)
        weighted = weighted * rescale[:, :, None] + jnp.einsum(
            "hqk,khd->hqd",
            weights.astype(jnp.bfloat16),
            value_block,
            preferred_element_type=jnp.float32,
        )
        return ((new_max, row_sum, weighted), None)

    result_state, unused = lax.scan(
        one_step, initial, (key_blocks, value_blocks, key_nodes, key_valid)
    )
    final_max, final_sum, final_weighted = result_state
    attention = (final_weighted / final_sum[:, :, None]).astype(jnp.bfloat16)
    attention = jnp.transpose(attention, (1, 0, 2)).reshape(queries_all, group_width)
    result = lax.psum_scatter(
        jnp.dot(attention, w_out, preferred_element_type=jnp.float32).astype(jnp.bfloat16),
        "head",
        scatter_dimension=0,
        tiled=True,
    )
    return result[None]


def solution(mesh):
    placed = (
        P("page", "head", None),
        P(),
        P(None, None, "head"),
        P("head", None),
        P(None, "page", None, "head"),
        P(),
        P(),
        P(),
        P("page", None),
        P("page", None),
    )
    return jax.shard_map(
        shards, mesh=mesh, in_specs=placed, out_specs=P("page", "head", None), check_vma=False
    )
```

profile of v0, /device:TPU:1, one launch (start us, length us, event | category | flops | bytes accessed | tf_op | source)
XLA Modules:
  0.0 339.6 jit_solution(15440758614901769843)
XLA Ops:
  16.4 27.6 %all-gather.3.cloned.1.call-done = bf16[1024,1024]{1,0:T(8,128)(2,1)} async-done(((bf16[256,1024]{1,0:T(8,128)(2,1)}), bf16[1024,1024]{1,0:T(8,128)(2,1)}) %all-gather.3.cloned.1.call-update) | async-done | bytes 2097168 | tf_op jit(solution)/shard_map/all_gather | solution.py:41
  48.4 24.0 %while.30 = (s32[]{:T(128)}, f32[2,4,512]{2,1,0:T(4,128)S(1)}, f32[2,4,512]{2,1,0:T(4,128)S(1)}, f32[2,4,512,64]{2,3,1,0:T(8,128)S(1)}, s32[2]{0:T(128)S(1)}, /*...) while((s32[]{:T(128)}, f32[2,4,512]{2,1,0:T(4,128)S(1)}, ...), condition=%wide.region_4.5_spmd.clone, body=%wide.region_1.4_spmd.clone.sunk | while | flops 565703168 | bytes 29178048 | solution.py:83
  72.5 27.1 %all-gather.5.cloned.1.call-done = bf16[2,64,128,256]{3,2,1,0:T(8,128)(2,1)} async-done(((bf16[2,2,128,256]{3,2,1,0:T(8,128)(2,1)}), bf16[2,64,128,256]{3,2,1,0:T(8,128)(2,1)}) %all-gather.5.cloned.1.call-update) | async-done | bytes 8388624 | tf_op jit(solution)/shard_map/all_gather | solution.py:91
  99.5 6.0 %fusion.43 = (bf16[1,64,128,256]{3,2,1,0:T(8,128)(2,1)}, bf16[1,64,128,256]{3,2,1,0:T(8,128)(2,1)}) fusion(bf16[2,64,128,256]{3,2,1,0:T(8,128)(2,1)} %all-gather.5.cloned.1.call-done), kind=kLoop, calls=%fused_computation.63 | loop fusion | bytes 16777216 | tf_op jit(solution)/shard_map/slice | solution.py:97
  105.5 12.9 %reshape.224 = bf16[16,512,4,64]{3,2,1,0:T(4,128)(2,1)} reshape(bf16[1,64,128,256]{3,2,1,0:T(8,128)(2,1)} %get-tuple-element.231) | data formatting | bytes 8388608 | tf_op jit(solution)/shard_map/reshape;squeeze | solution.py:96
  118.4 12.7 %copy.24 = bf16[16,512,4,64]{1,3,2,0:T(8,128)(2,1)} copy(bf16[16,512,4,64]{3,2,1,0:T(4,128)(2,1)} %reshape.224) | data formatting | bytes 8388608 | tf_op jit(solution)/shard_map/while | solution.py:126
  131.1 12.9 %reshape.225 = bf16[16,512,4,64]{3,2,1,0:T(4,128)(2,1)} reshape(bf16[1,64,128,256]{3,2,1,0:T(8,128)(2,1)} %get-tuple-element.230) | data formatting | bytes 8388608 | tf_op jit(solution)/shard_map/reshape;squeeze | solution.py:97
  144.0 12.7 %copy.25 = bf16[16,512,4,64]{1,3,2,0:T(8,128)(2,1)} copy(bf16[16,512,4,64]{3,2,1,0:T(4,128)(2,1)} %reshape.225) | data formatting | bytes 8388608 | tf_op jit(solution)/shard_map/while | solution.py:126
  156.7 145.0 %while.29 = (s32[]{:T(128)}, f32[4,1024]{1,0:T(4,128)S(1)}, f32[4,1024]{1,0:T(4,128)S(1)}, f32[4,1024,64]{1,2,0:T(8,128)S(1)}, s32[16,512]{1,0:T(8,128)S(1)}, /*...) while((s32[]{:T(128)}, f32[4,1024]{1,0:T(4,128)S(1)}, ...), condition=%wide.region_11.12_spmd, body=%wide.region_8.11_spmd.sunk | while | flops 567812096 | bytes 30691972 | solution.py:126
  162.0 3.6 %fusion.70 = f32[4,1024,64]{1,2,0:T(8,128)S(1)} fusion(f32[4,512,1024]{2,1,0:T(8,128)S(1)} %get-tuple-element.368, f32[4,1024]{1,0:T(4,128)S(1)} %max.4, pred[1024,512]{0,1:T(8,128)(4,1)S(1)} %or_and_fusion.2, f32[4,1024,64]{1,2,0:T(8,128)S(1)} %get-tuple-element.440, f32[4,1024]{1,0:T(4,128)S(1)} %get-tuple-element.370, ...), kind=kOutput, calls=%fused_computation.29.clone.1 | convolution fusion | flops 279445504 | bytes 11305472 | tf_op jit(solution)/shard_map/while/body/eval_jaxpr/hqk,khd->hqd/dot_general | solution.py:118
  171.1 3.6 %fusion.70 = f32[4,1024,64]{1,2,0:T(8,128)S(1)} fusion(f32[4,512,1024]{2,1,0:T(8,128)S(1)} %get-tuple-element.368, f32[4,1024]{1,0:T(4,128)S(1)} %max.4, pred[1024,512]{0,1:T(8,128)(4,1)S(1)} %or_and_fusion.2, f32[4,1024,64]{1,2,0:T(8,128)S(1)} %get-tuple-element.440, f32[4,1024]{1,0:T(4,128)S(1)} %get-tuple-element.370, ...), kind=kOutput, calls=%fused_computation.29.clone.1 | convolution fusion | flops 279445504 | bytes 11305472 | tf_op jit(solution)/shard_map/while/body/eval_jaxpr/hqk,khd->hqd/dot_general | solution.py:118
  180.2 3.6 %fusion.70 = f32[4,1024,64]{1,2,0:T(8,128)S(1)} fusion(f32[4,512,1024]{2,1,0:T(8,128)S(1)} %get-tuple-element.368, f32[4,1024]{1,0:T(4,128)S(1)} %max.4, pred[1024,512]{0,1:T(8,128)(4,1)S(1)} %or_and_fusion.2, f32[4,1024,64]{1,2,0:T(8,128)S(1)} %get-tuple-element.440, f32[4,1024]{1,0:T(4,128)S(1)} %get-tuple-element.370, ...), kind=kOutput, calls=%fused_computation.29.clone.1 | convolution fusion | flops 279445504 | bytes 11305472 | tf_op jit(solution)/shard_map/while/body/eval_jaxpr/hqk,khd->hqd/dot_general | solution.py:118
  189.2 3.6 %fusion.70 = f32[4,1024,64]{1,2,0:T(8,128)S(1)} fusion(f32[4,512,1024]{2,1,0:T(8,128)S(1)} %get-tuple-element.368, f32[4,1024]{1,0:T(4,128)S(1)} %max.4, pred[1024,512]{0,1:T(8,128)(4,1)S(1)} %or_and_fusion.2, f32[4,1024,64]{1,2,0:T(8,128)S(1)} %get-tuple-element.440, f32[4,1024]{1,0:T(4,128)S(1)} %get-tuple-element.370, ...), kind=kOutput, calls=%fused_computation.29.clone.1 | convolution fusion | flops 279445504 | bytes 11305472 | tf_op jit(solution)/shard_map/while/body/eval_jaxpr/hqk,khd->hqd/dot_general | solution.py:118
  198.3 3.6 %fusion.70 = f32[4,1024,64]{1,2,0:T(8,128)S(1)} fusion(f32[4,512,1024]{2,1,0:T(8,128)S(1)} %get-tuple-element.368, f32[4,1024]{1,0:T(4,128)S(1)} %max.4, pred[1024,512]{0,1:T(8,128)(4,1)S(1)} %or_and_fusion.2, f32[4,1024,64]{1,2,0:T(8,128)S(1)} %get-tuple-element.440, f32[4,1024]{1,0:T(4,128)S(1)} %get-tuple-element.370, ...), kind=kOutput, calls=%fused_computation.29.clone.1 | convolution fusion | flops 279445504 | bytes 11305472 | tf_op jit(solution)/shard_map/while/body/eval_jaxpr/hqk,khd->hqd/dot_general | solution.py:118
  207.4 3.6 %fusion.70 = f32[4,1024,64]{1,2,0:T(8,128)S(1)} fusion(f32[4,512,1024]{2,1,0:T(8,128)S(1)} %get-tuple-element.368, f32[4,1024]{1,0:T(4,128)S(1)} %max.4, pred[1024,512]{0,1:T(8,128)(4,1)S(1)} %or_and_fusion.2, f32[4,1024,64]{1,2,0:T(8,128)S(1)} %get-tuple-element.440, f32[4,1024]{1,0:T(4,128)S(1)} %get-tuple-element.370, ...), kind=kOutput, calls=%fused_computation.29.clone.1 | convolution fusion | flops 279445504 | bytes 11305472 | tf_op jit(solution)/shard_map/while/body/eval_jaxpr/hqk,khd->hqd/dot_general | solution.py:118
  216.4 3.6 %fusion.70 = f32[4,1024,64]{1,2,0:T(8,128)S(1)} fusion(f32[4,512,1024]{2,1,0:T(8,128)S(1)} %get-tuple-element.368, f32[4,1024]{1,0:T(4,128)S(1)} %max.4, pred[1024,512]{0,1:T(8,128)(4,1)S(1)} %or_and_fusion.2, f32[4,1024,64]{1,2,0:T(8,128)S(1)} %get-tuple-element.440, f32[4,1024]{1,0:T(4,128)S(1)} %get-tuple-element.370, ...), kind=kOutput, calls=%fused_computation.29.clone.1 | convolution fusion | flops 279445504 | bytes 11305472 | tf_op jit(solution)/shard_map/while/body/eval_jaxpr/hqk,khd->hqd/dot_general | solution.py:118
  225.5 3.6 %fusion.70 = f32[4,1024,64]{1,2,0:T(8,128)S(1)} fusion(f32[4,512,1024]{2,1,0:T(8,128)S(1)} %get-tuple-element.368, f32[4,1024]{1,0:T(4,128)S(1)} %max.4, pred[1024,512]{0,1:T(8,128)(4,1)S(1)} %or_and_fusion.2, f32[4,1024,64]{1,2,0:T(8,128)S(1)} %get-tuple-element.440, f32[4,1024]{1,0:T(4,128)S(1)} %get-tuple-element.370, ...), kind=kOutput, calls=%fused_computation.29.clone.1 | convolution fusion | flops 279445504 | bytes 11305472 | tf_op jit(solution)/shard_map/while/body/eval_jaxpr/hqk,khd->hqd/dot_general | solution.py:118
  234.5 3.6 %fusion.70 = f32[4,1024,64]{1,2,0:T(8,128)S(1)} fusion(f32[4,512,1024]{2,1,0:T(8,128)S(1)} %get-tuple-element.368, f32[4,1024]{1,0:T(4,128)S(1)} %max.4, pred[1024,512]{0,1:T(8,128)(4,1)S(1)} %or_and_fusion.2, f32[4,1024,64]{1,2,0:T(8,128)S(1)} %get-tuple-element.440, f32[4,1024]{1,0:T(4,128)S(1)} %get-tuple-element.370, ...), kind=kOutput, calls=%fused_computation.29.clone.1 | convolution fusion | flops 279445504 | bytes 11305472 | tf_op jit(solution)/shard_map/while/body/eval_jaxpr/hqk,khd->hqd/dot_general | solution.py:118
  243.6 3.6 %fusion.70 = f32[4,1024,64]{1,2,0:T(8,128)S(1)} fusion(f32[4,512,1024]{2,1,0:T(8,128)S(1)} %get-tuple-element.368, f32[4,1024]{1,0:T(4,128)S(1)} %max.4, pred[1024,512]{0,1:T(8,128)(4,1)S(1)} %or_and_fusion.2, f32[4,1024,64]{1,2,0:T(8,128)S(1)} %get-tuple-element.440, f32[4,1024]{1,0:T(4,128)S(1)} %get-tuple-element.370, ...), kind=kOutput, calls=%fused_computation.29.clone.1 | convolution fusion | flops 279445504 | bytes 11305472 | tf_op jit(solution)/shard_map/while/body/eval_jaxpr/hqk,khd->hqd/dot_general | solution.py:118
  252.7 3.6 %fusion.70 = f32[4,1024,64]{1,2,0:T(8,128)S(1)} fusion(f32[4,512,1024]{2,1,0:T(8,128)S(1)} %get-tuple-element.368, f32[4,1024]{1,0:T(4,128)S(1)} %max.4, pred[1024,512]{0,1:T(8,128)(4,1)S(1)} %or_and_fusion.2, f32[4,1024,64]{1,2,0:T(8,128)S(1)} %get-tuple-element.440, f32[4,1024]{1,0:T(4,128)S(1)} %get-tuple-element.370, ...), kind=kOutput, calls=%fused_computation.29.clone.1 | convolution fusion | flops 279445504 | bytes 11305472 | tf_op jit(solution)/shard_map/while/body/eval_jaxpr/hqk,khd->hqd/dot_general | solution.py:118
  261.7 3.6 %fusion.70 = f32[4,1024,64]{1,2,0:T(8,128)S(1)} fusion(f32[4,512,1024]{2,1,0:T(8,128)S(1)} %get-tuple-element.368, f32[4,1024]{1,0:T(4,128)S(1)} %max.4, pred[1024,512]{0,1:T(8,128)(4,1)S(1)} %or_and_fusion.2, f32[4,1024,64]{1,2,0:T(8,128)S(1)} %get-tuple-element.440, f32[4,1024]{1,0:T(4,128)S(1)} %get-tuple-element.370, ...), kind=kOutput, calls=%fused_computation.29.clone.1 | convolution fusion | flops 279445504 | bytes 11305472 | tf_op jit(solution)/shard_map/while/body/eval_jaxpr/hqk,khd->hqd/dot_general | solution.py:118
  270.8 3.6 %fusion.70 = f32[4,1024,64]{1,2,0:T(8,128)S(1)} fusion(f32[4,512,1024]{2,1,0:T(8,128)S(1)} %get-tuple-element.368, f32[4,1024]{1,0:T(4,128)S(1)} %max.4, pred[1024,512]{0,1:T(8,128)(4,1)S(1)} %or_and_fusion.2, f32[4,1024,64]{1,2,0:T(8,128)S(1)} %get-tuple-element.440, f32[4,1024]{1,0:T(4,128)S(1)} %get-tuple-element.370, ...), kind=kOutput, calls=%fused_computation.29.clone.1 | convolution fusion | flops 279445504 | bytes 11305472 | tf_op jit(solution)/shard_map/while/body/eval_jaxpr/hqk,khd->hqd/dot_general | solution.py:118
  298.0 3.6 %fusion.70 = f32[4,1024,64]{1,2,0:T(8,128)S(1)} fusion(f32[4,512,1024]{2,1,0:T(8,128)S(1)} %get-tuple-element.368, f32[4,1024]{1,0:T(4,128)S(1)} %max.4, pred[1024,512]{0,1:T(8,128)(4,1)S(1)} %or_and_fusion.2, f32[4,1024,64]{1,2,0:T(8,128)S(1)} %get-tuple-element.440, f32[4,1024]{1,0:T(4,128)S(1)} %get-tuple-element.370, ...), kind=kOutput, calls=%fused_computation.29.clone.1 | convolution fusion | flops 279445504 | bytes 11305472 | tf_op jit(solution)/shard_map/while/body/eval_jaxpr/hqk,khd->hqd/dot_general | solution.py:118
  303.9 29.2 %reduce-scatter.2.cloned.1.call-done = bf16[256,1024]{1,0:T(8,128)(2,1)} async-done(((bf16[1024,1024]{1,0:T(8,128)(2,1)}), bf16[256,1024]{1,0:T(8,128)(2,1)}) %reduce-scatter.2.cloned.1.call-update) | async-done | bytes 524304 | tf_op jit(solution)/shard_map/reduce_scatter | solution.py:132
  (179 shorter events, 129.7 us)
Async XLA Ops:
  6.5 295.2 %copy-start = (bf16[256,1024]{1,0:T(8,128)(2,1)S(1)}, bf16[256,1024]{1,0:T(8,128)(2,1)}, u32[]{:S(2)}) copy-start(bf16[256,1024]{1,0:T(8,128)(2,1)} %param.17) | copy-start | bytes 1572868
  6.5 37.5 %all-gather.3.cloned.1.call-start = ((), (), s32[]{:S(2)}) async-start(), calls=%async_computation.1 | async-start | bytes 2621440 | tf_op jit(solution)/shard_map/all_gather | solution.py:41
  9.9 89.7 %all-gather.5.cloned.1.call-start = ((), (), s32[]{:S(2)}) async-start(), calls=%async_computation.2 | async-start | bytes 8650752 | tf_op jit(solution)/shard_map/all_gather | solution.py:91
  10.6 322.5 %reduce-scatter.2.cloned.1.call-start = ((), (), s32[]{:S(2)}) async-start(), calls=%async_computation.3 | async-start | bytes 2621440 | tf_op jit(solution)/shard_map/reduce_scatter | solution.py:132
  10.7 37.7 %copy-start.1 = (s32[1,1024]{1,0:T(1,128)S(1)}, s32[1,1024]{1,0:T(1,128)}, u32[]{:S(2)}) copy-start(s32[1,1024]{1,0:T(1,128)} %param.22) | copy-start | bytes 12292
Sparse Core Ops, SparseCore 0:
  10.0 34.0 all-gather.2
  46.4 53.0 all-gather.4
  304.0 29.0 reduce-scatter.1
where the time goes:
time: 342 us; the launch traced here: 340 us
  matrix products  116 us (34%)
  waiting for transfers between devices  84.7 us (25%)
  local copies, waits for them, and re-layouts  63.5 us (19%)
  other arithmetic  57.9 us (17%)
  between operations  13.2 us (4%)
  loops' own time  4.56 us (1%)
    dot_general x16, matrix products, one_step(): jnp.einsum('hqk,khd->hqd', weights.astype(jnp.bfloat16), value_block, pre...  58.4 us
    dot_general x16, matrix products, one_step(): jnp.einsum('qhd,khd->hqk', queries, key_block, preferred_element_type=jnp...  40.8 us
    reduce_sum x16, other arithmetic, one_step(): row_sum = row_sum * rescale + jnp.sum(weights, axis=2)  33.7 us
    reduce_scatter x1, waiting for transfers between devices, shards(): lax.psum_scatter(jnp.dot(attention, w_out, preferred_element_type=jnp.flo...  29.2 us
    all_gather x1, waiting for transfers between devices, shards(): lax.all_gather(normed, 'head', axis=0, tiled=True)  27.6 us
    all_gather x1, waiting for transfers between devices, shards(): shard_piece = lax.all_gather(cache_kv, 'page', axis=1, tiled=True)  27.1 us
    while x2, local copies, waits for them, and re-layouts, shards(): lax.scan(one_step, initial, (key_blocks, value_blocks, key_nodes, key_val...  25.4 us
    another operation x1, local copies, waits for them, and re-layouts, shards(): shard_piece[0].reshape(step_count, block_keys, group_heads, head_size)  12.9 us
  transfers between devices with their start and end apart: 3, of which 3 were waited for; matrix products, arithmetic and copies ran while one was open for 9% of the time, Pallas kernels for 0%

commit v1 on v0

--- a/solution.py
+++ b/solution.py
@@ -7,6 +7,32 @@
 HD = 64
 EPSILON = 1e-06
 FLOOR_SCORE = -1e30
+
+
+def take_row_over_axis(xx):
+    steps_seen = []
+    b = 0
+    chips = lax.axis_size("head")
+    while b < chips:
+        steps_seen.append((b, (b + 1) % chips))
+        b += 1
+    b = 0
+    buffer = []
+    while b < chips:
+        buffer.append((b, (b - 1) % chips))
+        b += 1
+    base_arr, high = ([xx], [xx])
+    for _ in range(chips // 2):
+        base_arr.append(lax.ppermute(base_arr[-1], "head", steps_seen))
+    ix = 0
+    while ix < (chips - 1) // 2:
+        high.append(lax.ppermute(high[-1], "head", buffer))
+        ix = ix + 1
+    return jnp.roll(
+        jnp.concatenate([*base_arr[::-1], *high[1:]], 0),
+        (lax.axis_index("head") - chips // 2) * xx.shape[0],
+        0,
+    )
 
 
 def lookup(indices, lookup_table):
@@ -38,9 +64,7 @@
     group_heads = group_width // head_size
     weight_flat = w_qkv.reshape(model_width, 3 * group_width)
     projected = jnp.dot(
-        lax.all_gather(normed, "head", axis=0, tiled=True),
-        weight_flat,
-        preferred_element_type=jnp.float32,
+        take_row_over_axis(normed), weight_flat, preferred_element_type=jnp.float32
     ).astype(jnp.bfloat16)
     queries_all = projected.shape[0]
     queries = projected[:, :group_width].reshape(queries_all, group_heads, head_size)

time: 342 us -> 311 us (0.909)
  waiting for transfers between devices: 84.7 us -> 50 us
  starting transfers between devices: 0.08 us -> 4.8 us
    all_gather x1 -> x0, waiting for transfers between devices: 27.6 us -> none  [shards(): lax.all_gather(normed, 'head', axis=0, tiled=True)]
    all_gather x1, waiting for transfers between devices: 27.1 us -> 0.02 us  [shards(): shard_piece = lax.all_gather(cache_kv, 'page', axis=1, tiled=True)]
    ppermute x0 -> x3, waiting for transfers between devices: none -> 18.9 us  [the longest x2 18.9 us: take_row_over_axis(): base_arr.append(lax.ppermute(base_arr[-1], 'head', steps_seen))]
    ppermute x0 -> x3, starting transfers between devices: none -> 4.73 us  [the longest x2 2.53 us: take_row_over_axis(): base_arr.append(lax.ppermute(base_arr[-1], 'head', steps_seen))]
  transfers between devices with their start and end apart: 3 -> 5, of which waited for: 3 -> 3; matrix products, arithmetic and copies ran while one was open for 9% -> 10% of each run, Pallas kernels for 0% -> 0%
where the time goes in v1:
time: 311 us; the launch traced here: 309 us
  matrix products  114 us (37%)
  local copies, waits for them, and re-layouts  64.4 us (21%)
  other arithmetic  57.4 us (18%)
  waiting for transfers between devices  50 us (16%)
  between operations  13.7 us (4%)
  starting transfers between devices  4.8 us (2%)
  loops' own time  4.57 us (1%)
    dot_general x16, matrix products, one_step(): jnp.einsum('hqk,khd->hqd', weights.astype(jnp.bfloat16), value_block, pre...  58.3 us
    dot_general x16, matrix products, one_step(): jnp.einsum('qhd,khd->hqk', queries, key_block, preferred_element_type=jnp...  40.8 us
    reduce_sum x16, other arithmetic, one_step(): row_sum = row_sum * rescale + jnp.sum(weights, axis=2)  33.7 us
    reduce_scatter x1, waiting for transfers between devices, shards(): lax.psum_scatter(jnp.dot(attention, w_out, preferred_element_type=jnp.flo...  30.4 us
    while x2, local copies, waits for them, and re-layouts, shards(): lax.scan(one_step, initial, (key_blocks, value_blocks, key_nodes, key_val...  25.4 us
    ppermute x2, waiting for transfers between devices, take_row_over_axis(): base_arr.append(lax.ppermute(base_arr[-1], 'head', steps_seen))  18.9 us
    another operation x1, local copies, waits for them, and re-layouts, shards(): shard_piece[0].reshape(step_count, block_keys, group_heads, head_size)  12.9 us
    another operation x1, local copies, waits for them, and re-layouts, shards(): shard_piece[1].reshape(step_count, block_keys, group_heads, head_size)  12.9 us
  transfers between devices with their start and end apart: 5, of which 3 were waited for; matrix products, arithmetic and copies ran while one was open for 10% of the time, Pallas kernels for 0%

profile of v1, /device:TPU:1, one launch (start us, length us, event | category | flops | bytes accessed | tf_op | source)
XLA Modules:
  0.0 308.6 jit_solution(9293489765851568614)
XLA Ops:
  16.8 9.3 %collective-permute-done = bf16[256,1024]{1,0:T(8,128)(2,1)S(1)} collective-permute-done((bf16[256,1024]{1,0:T(8,128)(2,1)S(1)}, bf16[256,1024]{1,0:T(8,128)(2,1)S(1)}, u32[]{:S(2)}, u32[]{:S(2)}) %collective-permute-start) | collective-permute-done | bytes 524320 | tf_op jit(solution)/shard_map/ppermute | solution.py:26
  29.8 9.7 %collective-permute-done.1 = bf16[256,1024]{1,0:T(8,128)(2,1)S(1)} collective-permute-done((bf16[256,1024]{1,0:T(8,128)(2,1)S(1)}, bf16[256,1024]{1,0:T(8,128)(2,1)S(1)}, u32[]{:S(2)}, u32[]{:S(2)}) %collective-permute-start.1) | collective-permute-done | bytes 524320 | tf_op jit(solution)/shard_map/ppermute | solution.py:26
  42.2 23.4 %while.30 = (s32[]{:T(128)}, f32[2,4,512]{2,1,0:T(4,128)S(1)}, f32[2,4,512]{2,1,0:T(4,128)S(1)}, f32[2,4,512,64]{2,3,1,0:T(8,128)}, s32[2]{0:T(128)S(1)}, /*inde...) while((s32[]{:T(128)}, f32[2,4,512]{2,1,0:T(4,128)S(1)}, ...), condition=%wide.region_4.5_spmd.clone, body=%wide.region_1.4_spmd.clone.sunk | while | flops 565703168 | bytes 29178556 | solution.py:107
  67.0 6.0 %fusion.49 = (bf16[1,64,128,256]{3,2,1,0:T(8,128)(2,1)}, bf16[1,64,128,256]{3,2,1,0:T(8,128)(2,1)}) fusion(bf16[2,64,128,256]{3,2,1,0:T(8,128)(2,1)} %all-gather.2.cloned.1.call-done), kind=kLoop, calls=%fused_computation.74 | loop fusion | bytes 16777216 | tf_op jit(solution)/shard_map/slice | solution.py:121
  73.0 12.9 %reshape.224 = bf16[16,512,4,64]{3,2,1,0:T(4,128)(2,1)} reshape(bf16[1,64,128,256]{3,2,1,0:T(8,128)(2,1)} %get-tuple-element.231) | data formatting | bytes 8388608 | tf_op jit(solution)/shard_map/reshape;squeeze | solution.py:120
  85.8 12.7 %copy.24 = bf16[16,512,4,64]{1,3,2,0:T(8,128)(2,1)} copy(bf16[16,512,4,64]{3,2,1,0:T(4,128)(2,1)} %reshape.224) | data formatting | bytes 8388608 | tf_op jit(solution)/shard_map/while | solution.py:150
  98.5 12.9 %reshape.225 = bf16[16,512,4,64]{3,2,1,0:T(4,128)(2,1)} reshape(bf16[1,64,128,256]{3,2,1,0:T(8,128)(2,1)} %get-tuple-element.230) | data formatting | bytes 8388608 | tf_op jit(solution)/shard_map/reshape;squeeze | solution.py:121
  111.4 12.7 %copy.25 = bf16[16,512,4,64]{1,3,2,0:T(8,128)(2,1)} copy(bf16[16,512,4,64]{3,2,1,0:T(4,128)(2,1)} %reshape.225) | data formatting | bytes 8388608 | tf_op jit(solution)/shard_map/while | solution.py:150
  124.1 145.0 %while.29 = (s32[]{:T(128)}, f32[4,1024]{1,0:T(4,128)S(1)}, f32[4,1024]{1,0:T(4,128)S(1)}, f32[4,1024,64]{1,2,0:T(8,128)S(1)}, s32[16,512]{1,0:T(8,128)S(1)}, /*...) while((s32[]{:T(128)}, f32[4,1024]{1,0:T(4,128)S(1)}, ...), condition=%wide.region_11.12_spmd, body=%wide.region_8.11_spmd.sunk | while | flops 567812096 | bytes 30691972 | solution.py:150
  129.5 3.6 %fusion.75 = f32[4,1024,64]{1,2,0:T(8,128)S(1)} fusion(f32[4,512,1024]{2,1,0:T(8,128)S(1)} %get-tuple-element.368, f32[4,1024]{1,0:T(4,128)S(1)} %max.4, pred[1024,512]{0,1:T(8,128)(4,1)S(1)} %or_and_fusion.2, f32[4,1024,64]{1,2,0:T(8,128)S(1)} %get-tuple-element.440, f32[4,1024]{1,0:T(4,128)S(1)} %get-tuple-element.370, ...), kind=kOutput, calls=%fused_computation.29.clone.1 | convolution fusion | flops 279445504 | bytes 11305472 | tf_op jit(solution)/shard_map/while/body/eval_jaxpr/hqk,khd->hqd/dot_general | solution.py:142
  138.6 3.6 %fusion.75 = f32[4,1024,64]{1,2,0:T(8,128)S(1)} fusion(f32[4,512,1024]{2,1,0:T(8,128)S(1)} %get-tuple-element.368, f32[4,1024]{1,0:T(4,128)S(1)} %max.4, pred[1024,512]{0,1:T(8,128)(4,1)S(1)} %or_and_fusion.2, f32[4,1024,64]{1,2,0:T(8,128)S(1)} %get-tuple-element.440, f32[4,1024]{1,0:T(4,128)S(1)} %get-tuple-element.370, ...), kind=kOutput, calls=%fused_computation.29.clone.1 | convolution fusion | flops 279445504 | bytes 11305472 | tf_op jit(solution)/shard_map/while/body/eval_jaxpr/hqk,khd->hqd/dot_general | solution.py:142
  147.6 3.6 %fusion.75 = f32[4,1024,64]{1,2,0:T(8,128)S(1)} fusion(f32[4,512,1024]{2,1,0:T(8,128)S(1)} %get-tuple-element.368, f32[4,1024]{1,0:T(4,128)S(1)} %max.4, pred[1024,512]{0,1:T(8,128)(4,1)S(1)} %or_and_fusion.2, f32[4,1024,64]{1,2,0:T(8,128)S(1)} %get-tuple-element.440, f32[4,1024]{1,0:T(4,128)S(1)} %get-tuple-element.370, ...), kind=kOutput, calls=%fused_computation.29.clone.1 | convolution fusion | flops 279445504 | bytes 11305472 | tf_op jit(solution)/shard_map/while/body/eval_jaxpr/hqk,khd->hqd/dot_general | solution.py:142
  156.7 3.6 %fusion.75 = f32[4,1024,64]{1,2,0:T(8,128)S(1)} fusion(f32[4,512,1024]{2,1,0:T(8,128)S(1)} %get-tuple-element.368, f32[4,1024]{1,0:T(4,128)S(1)} %max.4, pred[1024,512]{0,1:T(8,128)(4,1)S(1)} %or_and_fusion.2, f32[4,1024,64]{1,2,0:T(8,128)S(1)} %get-tuple-element.440, f32[4,1024]{1,0:T(4,128)S(1)} %get-tuple-element.370, ...), kind=kOutput, calls=%fused_computation.29.clone.1 | convolution fusion | flops 279445504 | bytes 11305472 | tf_op jit(solution)/shard_map/while/body/eval_jaxpr/hqk,khd->hqd/dot_general | solution.py:142
  165.7 3.6 %fusion.75 = f32[4,1024,64]{1,2,0:T(8,128)S(1)} fusion(f32[4,512,1024]{2,1,0:T(8,128)S(1)} %get-tuple-element.368, f32[4,1024]{1,0:T(4,128)S(1)} %max.4, pred[1024,512]{0,1:T(8,128)(4,1)S(1)} %or_and_fusion.2, f32[4,1024,64]{1,2,0:T(8,128)S(1)} %get-tuple-element.440, f32[4,1024]{1,0:T(4,128)S(1)} %get-tuple-element.370, ...), kind=kOutput, calls=%fused_computation.29.clone.1 | convolution fusion | flops 279445504 | bytes 11305472 | tf_op jit(solution)/shard_map/while/body/eval_jaxpr/hqk,khd->hqd/dot_general | solution.py:142
  174.8 3.6 %fusion.75 = f32[4,1024,64]{1,2,0:T(8,128)S(1)} fusion(f32[4,512,1024]{2,1,0:T(8,128)S(1)} %get-tuple-element.368, f32[4,1024]{1,0:T(4,128)S(1)} %max.4, pred[1024,512]{0,1:T(8,128)(4,1)S(1)} %or_and_fusion.2, f32[4,1024,64]{1,2,0:T(8,128)S(1)} %get-tuple-element.440, f32[4,1024]{1,0:T(4,128)S(1)} %get-tuple-element.370, ...), kind=kOutput, calls=%fused_computation.29.clone.1 | convolution fusion | flops 279445504 | bytes 11305472 | tf_op jit(solution)/shard_map/while/body/eval_jaxpr/hqk,khd->hqd/dot_general | solution.py:142
  183.9 3.6 %fusion.75 = f32[4,1024,64]{1,2,0:T(8,128)S(1)} fusion(f32[4,512,1024]{2,1,0:T(8,128)S(1)} %get-tuple-element.368, f32[4,1024]{1,0:T(4,128)S(1)} %max.4, pred[1024,512]{0,1:T(8,128)(4,1)S(1)} %or_and_fusion.2, f32[4,1024,64]{1,2,0:T(8,128)S(1)} %get-tuple-element.440, f32[4,1024]{1,0:T(4,128)S(1)} %get-tuple-element.370, ...), kind=kOutput, calls=%fused_computation.29.clone.1 | convolution fusion | flops 279445504 | bytes 11305472 | tf_op jit(solution)/shard_map/while/body/eval_jaxpr/hqk,khd->hqd/dot_general | solution.py:142
  192.9 3.6 %fusion.75 = f32[4,1024,64]{1,2,0:T(8,128)S(1)} fusion(f32[4,512,1024]{2,1,0:T(8,128)S(1)} %get-tuple-element.368, f32[4,1024]{1,0:T(4,128)S(1)} %max.4, pred[1024,512]{0,1:T(8,128)(4,1)S(1)} %or_and_fusion.2, f32[4,1024,64]{1,2,0:T(8,128)S(1)} %get-tuple-element.440, f32[4,1024]{1,0:T(4,128)S(1)} %get-tuple-element.370, ...), kind=kOutput, calls=%fused_computation.29.clone.1 | convolution fusion | flops 279445504 | bytes 11305472 | tf_op jit(solution)/shard_map/while/body/eval_jaxpr/hqk,khd->hqd/dot_general | solution.py:142
  202.0 3.6 %fusion.75 = f32[4,1024,64]{1,2,0:T(8,128)S(1)} fusion(f32[4,512,1024]{2,1,0:T(8,128)S(1)} %get-tuple-element.368, f32[4,1024]{1,0:T(4,128)S(1)} %max.4, pred[1024,512]{0,1:T(8,128)(4,1)S(1)} %or_and_fusion.2, f32[4,1024,64]{1,2,0:T(8,128)S(1)} %get-tuple-element.440, f32[4,1024]{1,0:T(4,128)S(1)} %get-tuple-element.370, ...), kind=kOutput, calls=%fused_computation.29.clone.1 | convolution fusion | flops 279445504 | bytes 11305472 | tf_op jit(solution)/shard_map/while/body/eval_jaxpr/hqk,khd->hqd/dot_general | solution.py:142
  211.1 3.6 %fusion.75 = f32[4,1024,64]{1,2,0:T(8,128)S(1)} fusion(f32[4,512,1024]{2,1,0:T(8,128)S(1)} %get-tuple-element.368, f32[4,1024]{1,0:T(4,128)S(1)} %max.4, pred[1024,512]{0,1:T(8,128)(4,1)S(1)} %or_and_fusion.2, f32[4,1024,64]{1,2,0:T(8,128)S(1)} %get-tuple-element.440, f32[4,1024]{1,0:T(4,128)S(1)} %get-tuple-element.370, ...), kind=kOutput, calls=%fused_computation.29.clone.1 | convolution fusion | flops 279445504 | bytes 11305472 | tf_op jit(solution)/shard_map/while/body/eval_jaxpr/hqk,khd->hqd/dot_general | solution.py:142
  220.1 3.6 %fusion.75 = f32[4,1024,64]{1,2,0:T(8,128)S(1)} fusion(f32[4,512,1024]{2,1,0:T(8,128)S(1)} %get-tuple-element.368, f32[4,1024]{1,0:T(4,128)S(1)} %max.4, pred[1024,512]{0,1:T(8,128)(4,1)S(1)} %or_and_fusion.2, f32[4,1024,64]{1,2,0:T(8,128)S(1)} %get-tuple-element.440, f32[4,1024]{1,0:T(4,128)S(1)} %get-tuple-element.370, ...), kind=kOutput, calls=%fused_computation.29.clone.1 | convolution fusion | flops 279445504 | bytes 11305472 | tf_op jit(solution)/shard_map/while/body/eval_jaxpr/hqk,khd->hqd/dot_general | solution.py:142
  229.2 3.6 %fusion.75 = f32[4,1024,64]{1,2,0:T(8,128)S(1)} fusion(f32[4,512,1024]{2,1,0:T(8,128)S(1)} %get-tuple-element.368, f32[4,1024]{1,0:T(4,128)S(1)} %max.4, pred[1024,512]{0,1:T(8,128)(4,1)S(1)} %or_and_fusion.2, f32[4,1024,64]{1,2,0:T(8,128)S(1)} %get-tuple-element.440, f32[4,1024]{1,0:T(4,128)S(1)} %get-tuple-element.370, ...), kind=kOutput, calls=%fused_computation.29.clone.1 | convolution fusion | flops 279445504 | bytes 11305472 | tf_op jit(solution)/shard_map/while/body/eval_jaxpr/hqk,khd->hqd/dot_general | solution.py:142
  238.2 3.6 %fusion.75 = f32[4,1024,64]{1,2,0:T(8,128)S(1)} fusion(f32[4,512,1024]{2,1,0:T(8,128)S(1)} %get-tuple-element.368, f32[4,1024]{1,0:T(4,128)S(1)} %max.4, pred[1024,512]{0,1:T(8,128)(4,1)S(1)} %or_and_fusion.2, f32[4,1024,64]{1,2,0:T(8,128)S(1)} %get-tuple-element.440, f32[4,1024]{1,0:T(4,128)S(1)} %get-tuple-element.370, ...), kind=kOutput, calls=%fused_computation.29.clone.1 | convolution fusion | flops 279445504 | bytes 11305472 | tf_op jit(solution)/shard_map/while/body/eval_jaxpr/hqk,khd->hqd/dot_general | solution.py:142
  256.4 3.6 %fusion.75 = f32[4,1024,64]{1,2,0:T(8,128)S(1)} fusion(f32[4,512,1024]{2,1,0:T(8,128)S(1)} %get-tuple-element.368, f32[4,1024]{1,0:T(4,128)S(1)} %max.4, pred[1024,512]{0,1:T(8,128)(4,1)S(1)} %or_and_fusion.2, f32[4,1024,64]{1,2,0:T(8,128)S(1)} %get-tuple-element.440, f32[4,1024]{1,0:T(4,128)S(1)} %get-tuple-element.370, ...), kind=kOutput, calls=%fused_computation.29.clone.1 | convolution fusion | flops 279445504 | bytes 11305472 | tf_op jit(solution)/shard_map/while/body/eval_jaxpr/hqk,khd->hqd/dot_general | solution.py:142
  271.3 30.4 %reduce-scatter.2.cloned.1.call-done = bf16[256,1024]{1,0:T(8,128)(2,1)} async-done(((bf16[1024,1024]{1,0:T(8,128)(2,1)}), bf16[256,1024]{1,0:T(8,128)(2,1)}) %reduce-scatter.2.cloned.1.call-update) | async-done | bytes 524304 | tf_op jit(solution)/shard_map/reduce_scatter | solution.py:156
  (198 shorter events, 132.8 us)
Async XLA Ops:
  6.5 262.7 %copy-start = (bf16[256,1024]{1,0:T(8,128)(2,1)S(1)}, bf16[256,1024]{1,0:T(8,128)(2,1)}, u32[]{:S(2)}) copy-start(bf16[256,1024]{1,0:T(8,128)(2,1)} %param.17) | copy-start | bytes 1572868
  6.5 33.1 %copy-start.1 = (bf16[1,256,1024]{2,1,0:T(8,128)(2,1)S(1)}, bf16[1,256,1024]{2,1,0:T(8,128)(2,1)}, u32[]{:S(2)}) copy-start(bf16[1,256,1024]{2,1,0:T(8,128)(2,1)} %param.14) | copy-start | bytes 1572868
  6.5 33.1 %copy-start.4 = (f32[1024]{0:T(1024)S(1)}, f32[1024]{0:T(1024)}, u32[]{:S(2)}) copy-start(f32[1024]{0:T(1024)} %param.15) | copy-start | bytes 12292
  6.5 23.1 %copy-start.5 = (s32[64]{0:T(128)S(1)}, s32[64]{0:T(128)}, u32[]{:S(2)}) copy-start(s32[64]{0:T(128)} %param.19) | copy-start | bytes 772
  6.5 60.4 %all-gather.2.cloned.1.call-start = ((), (), s32[]{:S(2)}) async-start(), calls=%async_computation.1 | async-start | bytes 8650752 | tf_op jit(solution)/shard_map/all_gather | solution.py:115
  7.3 294.4 %reduce-scatter.2.cloned.1.call-start = ((), (), s32[]{:S(2)}) async-start(), calls=%async_computation.2 | async-start | bytes 2621440 | tf_op jit(solution)/shard_map/reduce_scatter | solution.py:156
  9.8 16.3 %collective-permute-start = (bf16[256,1024]{1,0:T(8,128)(2,1)S(1)}, bf16[256,1024]{1,0:T(8,128)(2,1)S(1)}, u32[]{:S(2)}, u32[]{:S(2)}) collective-permute-start(bf16[256,1024]{1,0:T(8,128)(2,1)S(1)} %fusion.47), channel_id=1, source_target_pairs={{0,32},{32,64},{64,96},{96,0},{1,33},{33,65},{65,97},{97,1},{2,34}... | collective-permute-start | bytes 1572872 | tf_op jit(solution)/shard_map/ppermute | solution.py:26
  12.3 27.5 %collective-permute-start.2 = (bf16[256,1024]{1,0:T(8,128)(2,1)S(1)}, bf16[256,1024]{1,0:T(8,128)(2,1)S(1)}, u32[]{:S(2)}, u32[]{:S(2)}) collective-permute-start(bf16[256,1024]{1,0:T(8,128)(2,1)S(1)} %fusion.47), channel_id=1, source_target_pairs={{0,96},{32,0},{64,32},{96,64},{1,97},{33,1},{65,33},{97,65},{2,98}... | collective-permute-start | bytes 1572872 | tf_op jit(solution)/shard_map/ppermute | solution.py:29
  26.1 13.4 %collective-permute-start.1 = (bf16[256,1024]{1,0:T(8,128)(2,1)S(1)}, bf16[256,1024]{1,0:T(8,128)(2,1)S(1)}, u32[]{:S(2)}, u32[]{:S(2)}) collective-permute-start(bf16[256,1024]{1,0:T(8,128)(2,1)S(1)} %collective-permute-done), channel_id=1, source_target_pairs={{0,32},{32,64},{64,96},{96,0},{1,33},{33,65},{65,97},{97,1},{2,34}... | collective-permute-start | bytes 1572872 | tf_op jit(solution)/shard_map/ppermute | solution.py:26
  29.8 10.4 %copy-start.2 = (bf16[1024,3,256]{0,2,1:T(8,128)(2,1)S(1)}, bf16[1024,3,256]{0,2,1:T(8,128)(2,1)}, u32[]{:S(2)}) copy-start(bf16[1024,3,256]{0,2,1:T(8,128)(2,1)} %copy.20) | copy-start | bytes 4718596
  40.2 2.0 copy-start.3
Sparse Core Ops, SparseCore 0:
  9.7 56.2 all-gather.1
  271.5 30.2 reduce-scatter.1
